TPU v7x, 128 devices: a whole 4x4x4 slice. The times are simulated.
128 devices in a mesh: req: 16 (over y, z), mlp: 8 (over x, core).
Axes of the slice: x: 4, y: 4, z: 4, core: 2. Of those that a mesh axis runs over, the one named last changes fastest.
Arguments:
- tokens: bfloat16 [32768, 1536], P(('req', 'mlp')), may hold values from -6 to 6
- attn_gain: float32 [1536], replicated, may hold values from 0.1 to 1.9
- w_query: bfloat16 [1536, 1536], replicated, may hold values from -0.15625 to 0.15625
- w_keyval: bfloat16 [1536, 256], replicated, may hold values from -0.15625 to 0.15625
- w_out: bfloat16 [1536, 1536], replicated, may hold values from -0.15625 to 0.15625
- ffn_gain: float32 [1536], replicated, may hold values from 0.1 to 1.9
- w_gate: bfloat16 [1536, 4608], P('req', 'mlp'), may hold values from -0.15625 to 0.15625
- w_up: bfloat16 [1536, 4608], P('req', 'mlp'), may hold values from -0.15625 to 0.15625
- w_down: bfloat16 [1536, 4608], P('req', 'mlp'), may hold values from -0.09375 to 0.09375
- prefix_kv: bfloat16 [2, 128, 512, 256], P(None, 'req'), may hold values from -60 to 60, as said below
- own_prefix: bfloat16 [16, 512, 256], P('req'), may hold values from -60 to 60, as said below
- leaf_parent: int32 [16], replicated, may hold values from 0 to 127
- node_parent: int32 [128], replicated, may hold values from 0 to 127
- seg_lengths: int32 [3, 128], replicated, may hold values from 1 to 512
Outputs:
- layer_out: bfloat16 [32768, 1536], P(('req', 'mlp'))
Inputs may be any that keep to these rules, and one draw needn't show every extreme that they name: `prefix_kv`: columns below 128 are keys, the rest values. `own_prefix`: columns below 128 are keys, the rest values.
All inputs are finite; a program needn't handle non-finite values.
Results may differ from a plain program's by a relative error of at most 0.018.
Values may be sent and summed in bfloat16 or wider, within the bound.
No kernel may reach another device: no remote copies, remote signals or barrier semaphores. Data moves between devices by JAX's collectives and lax.ppermute only.
A program may use at most 192 MiB of HBM per device.

v0:
```python
import jax
import jax.numpy as jnp
from jax import lax
from jax.sharding import PartitionSpec as P

HEADS = 12
HD = 128
WINDOW = 1024
EPS = 1e-06


def rms_scale(values, gain):
    wide = values.astype(jnp.float32)
    return wide * lax.rsqrt(jnp.mean(wide * wide, axis=-1, keepdims=True) + EPS) * gain


def rotate(values, where_at):
    half_dim = values.shape[-1] // 2
    freqs = 10000.0 ** (-jnp.arange(half_dim, dtype=jnp.float32) / half_dim)
    angles = where_at.astype(jnp.float32)[:, None] * freqs[None, :]
    cosine = jnp.cos(angles)[:, None, :]
    sine = jnp.sin(angles)[:, None, :]
    first = values[..., :half_dim]
    second = values[..., half_dim:]
    return jnp.concatenate([first * cosine - second * sine, first * sine + second * cosine], -1)


def attend(queries, piece, key_at, key_live, query_at):
    scores = jnp.einsum("thd,kd->thk", queries, piece[:, :HD], preferred_element_type=jnp.float32)
    spacing = query_at[:, None] - key_at[None, :]
    allowed = (key_live[None, :] & (spacing >= 0) & (spacing < WINDOW))[:, None, :]
    top = jnp.max(jnp.where(allowed, scores, -jnp.inf), axis=-1)
    safe_top = jnp.where(jnp.isfinite(top), top, 0.0)
    weights = jnp.where(allowed, jnp.exp(scores - safe_top[..., None]), 0.0)
    mixed = jnp.einsum(
        "thk,kd->thd",
        weights.astype(jnp.bfloat16),
        piece[:, HD:],
        preferred_element_type=jnp.float32,
    )
    return (top, jnp.sum(weights, axis=-1), mixed)


def combine(first, second):
    top = jnp.maximum(first[0], second[0])
    safe_top = jnp.where(jnp.isfinite(top), top, 0.0)
    scale_first = jnp.exp(first[0] - safe_top)
    scale_second = jnp.exp(second[0] - safe_top)
    denom = first[1] * scale_first + second[1] * scale_second
    mixed = first[2] * scale_first[..., None] + second[2] * scale_second[..., None]
    return (top, denom, mixed)


def body(
    tokens,
    attn_gain,
    w_query,
    w_keyval,
    w_out,
    ffn_gain,
    w_gate,
    w_up,
    w_down,
    prefix_kv,
    own_prefix,
    leaf_parent,
    node_parent,
    seg_lengths,
):
    tok_rows = tokens.shape[0]
    requests = lax.axis_size("req")
    mine = lax.axis_index("req")
    position_group = lax.axis_index("mlp")
    node_dev = prefix_kv.shape[1]
    seg_slot = prefix_kv.shape[2]
    leaf = leaf_parent[mine]
    upper = node_parent[leaf]
    len_zero = seg_lengths[0, upper]
    len_one = seg_lengths[1, leaf]
    len_two = seg_lengths[2, mine]
    total = len_zero + len_one + len_two
    query_at = total + position_group * tok_rows + jnp.arange(tok_rows, dtype=jnp.int32)
    normed = rms_scale(tokens, attn_gain).astype(jnp.bfloat16)
    query_full = jnp.dot(normed, w_query, preferred_element_type=jnp.float32).reshape(
        tok_rows, HEADS, HD
    )
    queries = (rotate(query_full, query_at) * HD ** (-0.5)).astype(jnp.bfloat16)
    keyval_full = jnp.dot(normed, w_keyval, preferred_element_type=jnp.float32)
    new_keys = rotate(keyval_full[:, None, :HD], query_at)[:, 0].astype(jnp.bfloat16)
    new_vals = keyval_full[:, HD:].astype(jnp.bfloat16)
    new_keyval = jnp.concatenate([new_keys, new_vals], 1)
    start_state = (
        jnp.full((tok_rows, HEADS), -jnp.inf, jnp.float32),
        jnp.zeros((tok_rows, HEADS), jnp.float32),
        jnp.zeros((tok_rows, HEADS, HD), jnp.float32),
    )
    piece = lax.all_gather(new_keyval, "mlp", axis=0, tiled=True)
    piece_at = total + jnp.arange(piece.shape[0], dtype=jnp.int32)
    live = jnp.ones((piece.shape[0],), dtype=bool)
    own_state = combine(start_state, attend(queries, piece, piece_at, live, query_at))
    level_zero = node_parent[leaf_parent]
    wanted = jnp.stack([level_zero, leaf_parent], 1)
    owned = wanted // node_dev == mine
    local_slot = wanted % node_dev
    picker = (
        (local_slot[:, :, None] == jnp.arange(node_dev, dtype=jnp.int32)[None, None, :])
        & owned[:, :, None]
    ).astype(jnp.bfloat16)
    owners = wanted[mine] // node_dev
    from_owner = (jnp.arange(requests, dtype=jnp.int32)[:, None] == owners[None, :]).astype(
        jnp.bfloat16
    )
    outgoing = jnp.einsum(
        "rln,lnsc->rlsc", picker, prefix_kv, preferred_element_type=jnp.float32
    ).astype(jnp.bfloat16)
    arrived = lax.all_to_all(outgoing, "req", split_axis=0, concat_axis=0, tiled=True)
    levels = jnp.einsum(
        "rl,rlsc->lsc", from_owner, arrived, preferred_element_type=jnp.float32
    ).astype(jnp.bfloat16)
    offsets = jnp.arange(seg_slot, dtype=jnp.int32)
    cached = jnp.concatenate([levels[0], levels[1], own_prefix[0]], 0)
    cached_at = jnp.concatenate([offsets, len_zero + offsets, len_zero + len_one + offsets], 0)
    cached_live = jnp.concatenate([offsets < len_zero, offsets < len_one, offsets < len_two], 0)
    merged = combine(own_state, attend(queries, cached, cached_at, cached_live, query_at))
    context = (merged[2] / merged[1][..., None]).reshape(tok_rows, HEADS * HD).astype(jnp.bfloat16)
    attn_out = jnp.dot(context, w_out, preferred_element_type=jnp.float32)
    resid = (tokens.astype(jnp.float32) + attn_out).astype(jnp.bfloat16)
    ffn_in = rms_scale(resid, ffn_gain).astype(jnp.bfloat16)
    all_rows = lax.all_gather(ffn_in, "mlp", axis=0, tiled=True)
    gate_full, up_full, down_full = (
        lax.all_gather(w_gate, "req", axis=0, tiled=True),
        lax.all_gather(w_up, "req", axis=0, tiled=True),
        lax.all_gather(w_down, "req", axis=0, tiled=True),
    )
    gate = jnp.dot(all_rows, gate_full, preferred_element_type=jnp.float32)
    upward = jnp.dot(all_rows, up_full, preferred_element_type=jnp.float32)
    hidden = (jax.nn.gelu(gate, approximate=True) * upward).astype(jnp.bfloat16)
    summed = lax.psum_scatter(
        lax.dot_general(
            hidden, down_full, (((1,), (1,)), ((), ())), preferred_element_type=jnp.float32
        ).astype(jnp.bfloat16),
        "mlp",
        scatter_dimension=0,
        tiled=True,
    ).astype(jnp.float32)
    return (resid.astype(jnp.float32) + summed).astype(jnp.bfloat16)


def solution(mesh):
    return jax.shard_map(
        body,
        mesh=mesh,
        in_specs=(
            P(("req", "mlp"), None),
            P(),
            P(),
            P(),
            P(),
            P(),
            P("req", "mlp"),
            P("req", "mlp"),
            P("req", "mlp"),
            P(None, "req", None, None),
            P("req", None, None),
            P(),
            P(),
            P(),
        ),
        out_specs=P(("req", "mlp"), None),
        check_vma=False,
    )
```

profile of v0, /device:TPU:1, one launch (start us, length us, event | category | flops | bytes accessed | tf_op | source)
XLA Modules:
  0.0 438.2 jit_solution(3613787128685627271)
XLA Ops:
  6.6 1.3 dynamic_slice.18
  9.8 1.2 dynamic_slice.19
  12.4 1.4 fusion.25
  13.8 1.7 fusion.35
  16.1 1.5 constant_dynamic-slice_fusion
  19.8 0.7 pad_maximum_fusion.1
  20.5 0.7 compare_select_fusion
  21.9 7.2 %convert_bitcast_fusion = bf16[16,2,512,256]{3,0,2,1:T(8,128)(2,1)} fusion(bf16[2,8,512,256]{3,2,1,0:T(8,128)(2,1)} %param.23, s32[16,2]{0,1:T(2,128)S(1)} %get-tuple-element.24, pred[16,2]{0,1:T(4,128)(4,1)S(1)} %fusion.54), kind=kOutput, calls=%fused_computation.15 | convolution fusion | flops 71303680 | bytes 12583072 | tf_op jit(solution)/shard_map/rln,lnsc->rlsc/dot_general | solution.py:113
  29.1 9.6 %copy.33 = bf16[16,2,512,256]{3,2,1,0:T(8,128)(2,1)} copy(bf16[16,2,512,256]{3,0,2,1:T(8,128)(2,1)} %convert_bitcast_fusion) | data formatting | bytes 16777216 | tf_op jit(solution)/shard_map/convert_element_type | solution.py:115
  38.8 8.9 %all-to-all-start = ((bf16[16,2,512,256]{3,2,1,0:T(8,128)(2,1)}), bf16[16,2,512,256]{3,2,1,0:T(8,128)(2,1)}, u32[]{:S(2)}, u32[]{:S(2)}) async-start(bf16[16,2,512,256]{3,2,1,0:T(8,128)(2,1)} %copy.33), calls=%async_computation | async-start | bytes 16777216 | tf_op jit(solution)/shard_map/all_to_all | solution.py:116
  47.7 0.7 all-gather.10.cloned.1.call-update
  48.8 4.3 fusion.37
  53.8 1.6 copy.44
  56.4 1.3 iota_compare_fusion.2
  58.8 1.9 multiply_subtract_fusion
  62.3 11.8 %select_reduce_fusion = (f32[256,12]{0,1:T(8,128)S(1)}, f32[256,12,2048]{2,0,1:T(8,128)}) fusion(pred[256,2048]{1,0:T(8,128)(4,1)S(1)} %fusion.24, bf16[256,12,128]{2,0,1:T(8,128)(2,1)S(1)} %fusion.28, bf16[2048,256]{0,1:T(8,128)(2,1)} %all-gather.6.cloned.1.call-done), kind=kOutput, calls=%fused_computation.2 | convolution fusion | flops 1623192576 | bytes 27013120 | tf_op jit(solution)/shard_map/thd,kd->thk/dot_general | solution.py:29
  74.2 11.3 %fusion = f32[256,12]{0,1:T(8,128)S(1)} fusion(f32[256,12,2048]{2,0,1:T(8,128)} %get-tuple-element.27, f32[256,12]{0,1:T(8,128)S(1)} %get-tuple-element.18, pred[256,2048]{1,0:T(8,128)(4,1)S(1)} %fusion.24), kind=kLoop, calls=%fused_computation.3 | loop fusion | flops 18871296 | bytes 25714688 | tf_op jit(solution)/shard_map/reduce_sum | solution.py:41
  85.5 11.8 %fusion.4 = f32[256,12,128]{0,2,1:T(8,128)} fusion(f32[256,12,2048]{2,0,1:T(8,128)} %get-tuple-element.27, f32[256,12]{0,1:T(8,128)S(1)} %get-tuple-element.18, pred[256,2048]{1,0:T(8,128)(4,1)S(1)} %fusion.24, bf16[2048,256]{0,1:T(8,128)(2,1)S(1)} %copy-done.5), kind=kOutput, calls=%fused_computation.9 | convolution fusion | flops 1629487104 | bytes 27803648 | tf_op jit(solution)/shard_map/thk,kd->thd/dot_general | solution.py:35
  97.3 97.6 %all-to-all-done = bf16[16,2,512,256]{3,2,1,0:T(8,128)(2,1)} async-done(((bf16[16,2,512,256]{3,2,1,0:T(8,128)(2,1)}), bf16[16,2,512,256]{3,2,1,0:T(8,128)(2,1)}, u32[]{:S(2)}, u32[]{:S(2)}) %all-to-all-start) | async-done | bytes 8388640 | tf_op jit(solution)/shard_map/all_to_all | solution.py:116
  194.9 8.3 %fusion.10 = bf16[2,1,512,256]{3,1,2,0:T(2,128)(2,1)S(1)} fusion(pred[16,2,1,1]{0,2,3,1:T(4,128)(4,1)S(1)} %copy.38, bf16[16,2,512,256]{3,2,1,0:T(8,128)(2,1)} %all-to-all-done), kind=kOutput, calls=%fused_computation.13 | convolution fusion | flops 8388608 | bytes 8912928 | tf_op jit(solution)/shard_map/rl,rlsc->lsc/dot_general | solution.py:117
  203.4 8.0 %select_reduce_fusion.1 = (f32[256,12]{0,1:T(8,128)S(1)}, f32[256,12,1536]{2,0,1:T(8,128)}) fusion(pred[256,1536]{1,0:T(8,128)(4,1)S(1)} %fusion.30, bf16[256,12,128]{2,0,1:T(8,128)(2,1)S(1)} %fusion.28, bf16[1536,256]{1,0:T(8,128)(2,1)S(1)} %pad_maximum_fusion), kind=kOutput, calls=%fused_computation.6 | convolution fusion | flops 1217393664 | bytes 20459520 | tf_op jit(solution)/shard_map/thd,kd->thk/dot_general | solution.py:29
  211.5 10.5 %fusion.2 = f32[256,12]{0,1:T(8,128)S(1)} fusion(f32[256,12,1536]{2,0,1:T(8,128)} %get-tuple-element.29, f32[256,12]{0,1:T(8,128)S(1)} %is-finite_select_fusion, pred[256,1536]{1,0:T(8,128)(4,1)S(1)} %fusion.30), kind=kLoop, calls=%fused_computation.7 | loop fusion | flops 14152704 | bytes 19292160 | tf_op jit(solution)/shard_map/reduce_sum | solution.py:41
  222.0 8.7 %divide_convert_fusion = bf16[256,12,128]{0,2,1:T(8,128)(2,1)S(1)} fusion(f32[256,12,128]{0,2,1:T(8,128)} %fusion.4, f32[256,12,1536]{2,0,1:T(8,128)} %get-tuple-element.29, f32[256,12]{0,1:T(8,128)S(1)} %is-finite_select_fusion, pred[256,1536]{1,0:T(8,128)(4,1)S(1)} %fusion.30, f32[256,12]{0,1:T(8,128)S(1)} %get-tuple-element.5, ...), kind=kOutput, calls=%fused_computation.46 | convolution fusion | flops 1224867840 | bytes 22118400 | tf_op jit(solution)/shard_map/thk,kd->thd/dot_general | solution.py:35
  230.8 1.5 multiply_reduce_fusion
  232.3 1.1 multiply_convert_fusion
  234.7 44.8 %all-gather.8.cloned.1.call-done = bf16[2048,1536]{1,0:T(8,128)(2,1)} async-done(((bf16[256,1536]{1,0:T(8,128)(2,1)}), bf16[2048,1536]{1,0:T(8,128)(2,1)}) %all-gather.8.cloned.1.call-update) | async-done | bytes 6291472 | tf_op jit(solution)/shard_map/all_gather | solution.py:129
  279.4 9.3 %fusion.63 = f32[2048,576]{0,1:T(8,128)} fusion(bf16[2048,1536]{1,0:T(8,128)(2,1)} %all-gather.8.cloned.1.call-done, bf16[1536,576]{1,0:T(8,128)(2,1)} %all-gather.10.cloned.1.call-done), kind=kOutput, calls=%fused_computation.133 | convolution fusion | flops 3623878656 | bytes 12779520 | tf_op jit(solution)/shard_map/dot_general | solution.py:135
  288.8 36.4 %all-gather.14.cloned.1.call-done = bf16[1536,576]{1,0:T(8,128)(2,1)} async-done(((bf16[96,576]{1,0:T(8,128)(2,1)}), bf16[1536,576]{1,0:T(8,128)(2,1)}) %all-gather.14.cloned.1.call-update) | async-done | bytes 1769488 | tf_op jit(solution)/shard_map/all_gather | solution.py:133
  325.2 46.1 %all-gather.12.cloned.1.call-done = bf16[1536,576]{1,0:T(8,128)(2,1)} async-done(((bf16[96,576]{1,0:T(8,128)(2,1)}), bf16[1536,576]{1,0:T(8,128)(2,1)}) %all-gather.12.cloned.1.call-update) | async-done | bytes 1769488 | tf_op jit(solution)/shard_map/all_gather | solution.py:132
  371.2 15.6 %convolution_convert_fusion = bf16[2048,1536]{1,0:T(8,128)(2,1)} fusion(bf16[1536,576]{1,0:T(8,128)(2,1)} %all-gather.14.cloned.1.call-done, f32[2048,576]{0,1:T(8,128)} %fusion.63, bf16[2048,1536]{1,0:T(8,128)(2,1)} %all-gather.8.cloned.1.call-done, bf16[1536,576]{1,0:T(8,128)(2,1)} %all-gather.12.cloned.1.call-done), kind=kOutput, calls=%fused_computation.16 | convolution fusion | flops 7262699520 | bytes 20840448 | tf_op jit(solution)/shard_map/dot_general | solution.py:139
  386.8 42.0 %reduce-scatter.2.cloned.1.call-done = bf16[256,1536]{1,0:T(8,128)(2,1)} async-done(((bf16[2048,1536]{1,0:T(8,128)(2,1)}), bf16[256,1536]{1,0:T(8,128)(2,1)}) %reduce-scatter.2.cloned.1.call-update) | async-done | bytes 786448 | tf_op jit(solution)/shard_map/reduce_scatter | solution.py:138
  428.9 2.2 add_convert_fusion
  (72 shorter events, 7.3 us)
Async XLA Ops:
  6.5 7.2 %copy-start = (bf16[1536,256]{1,0:T(8,128)(2,1)S(1)}, bf16[1536,256]{1,0:T(8,128)(2,1)}, u32[]{:S(2)}) copy-start(bf16[1536,256]{1,0:T(8,128)(2,1)} %param.17) | copy-start | bytes 2359300
  6.5 15.3 %copy-start.8 = (s32[16]{0:T(128)S(1)}, s32[16]{0:T(128)}, u32[]{:S(2)}) copy-start(s32[16]{0:T(128)} %param.25) | copy-start | bytes 196
  6.5 14.7 %copy-start.2 = (s32[128]{0:T(128)S(1)}, s32[128]{0:T(128)}, u32[]{:S(2)}) copy-start(s32[128]{0:T(128)} %param.26) | copy-start | bytes 1540
  6.5 55.8 %all-gather.6.cloned.1.call-start = ((), (), s32[]{:S(2)}) async-start(), calls=%async_computation.2 | async-start | bytes 1179648 | tf_op jit(solution)/shard_map/all_gather | solution.py:97
  38.8 10.0 %copy-start.3 = (bf16[256,1536]{1,0:T(8,128)(2,1)S(1)}, bf16[256,1536]{1,0:T(8,128)(2,1)}, u32[]{:S(2)}) copy-start(bf16[256,1536]{1,0:T(8,128)(2,1)} %param.14) | copy-start | bytes 2359300
  38.8 10.0 %copy-start.9 = (f32[1536]{0:T(1024)S(1)}, f32[1536]{0:T(1024)}, u32[]{:S(2)}) copy-start(f32[1536]{0:T(1024)} %param.15) | copy-start | bytes 18436
  38.8 156.1 %all-to-all-start = ((bf16[16,2,512,256]{3,2,1,0:T(8,128)(2,1)}), bf16[16,2,512,256]{3,2,1,0:T(8,128)(2,1)}, u32[]{:S(2)}, u32[]{:S(2)}) async-start(bf16[16,2,512,256]{3,2,1,0:T(8,128)(2,1)} %copy.33), calls=%async_computation | async-start | bytes 16777216 | tf_op jit(solution)/shard_map/all_to_all | solution.py:116
  47.7 187.0 %all-gather.10.cloned.1.call-start = ((), (), s32[]{:S(2)}) async-start(), calls=%async_computation.4 | async-start | bytes 2088960 | tf_op jit(solution)/shard_map/all_gather | solution.py:131
  48.4 231.0 %all-gather.8.cloned.1.call-start = ((), (), s32[]{:S(2)}) async-start(), calls=%async_computation.3 | async-start | bytes 7077888 | tf_op jit(solution)/shard_map/all_gather | solution.py:129
  74.2 11.4 %copy-start.5 = (bf16[2048,256]{0,1:T(8,128)(2,1)S(1)}, bf16[2048,256]{0,1:T(8,128)(2,1)}, u32[]{:S(2)}) copy-start(bf16[2048,256]{0,1:T(8,128)(2,1)} %all-gather.6.cloned.1.call-done) | copy-start | bytes 3145732
  97.3 106.0 %copy-start.6 = (bf16[1,512,256]{2,1,0:T(8,128)(2,1)S(1)}, bf16[1,512,256]{2,1,0:T(8,128)(2,1)}, u32[]{:S(2)}) copy-start(bf16[1,512,256]{2,1,0:T(8,128)(2,1)} %param.24) | copy-start | bytes 786436
  211.5 19.3 %slice-start = ((s8[4718592]{0:T(1024)(128)(4,1)}), s8[524288]{0:T(1024)(128)(4,1)S(1)}, s32[]{:S(2)}) async-start(s8[4718592]{0:T(1024)(128)(4,1)} %bitcast.58), calls=%async_computation.8 | async-start | bytes 1048576
  222.0 8.8 %slice-start.1 = ((s8[4718592]{0:T(1024)(128)(4,1)}), s8[4194304]{0:T(1024)(128)(4,1)S(1)}, s32[]{:S(2)}) async-start(s8[4718592]{0:T(1024)(128)(4,1)} %bitcast.58), calls=%async_computation.9 | async-start | bytes 8388608
  222.0 8.8 %copy-start.4 = (bf16[256,1536]{1,0:T(8,128)(2,1)S(1)}, bf16[256,1536]{1,0:T(8,128)(2,1)}, u32[]{:S(2)}) copy-start(bf16[256,1536]{1,0:T(8,128)(2,1)} %param.14) | copy-start | bytes 2359300
  230.8 1.5 copy-start.7
  233.4 91.7 %all-gather.14.cloned.1.call-start = ((), (), s32[]{:S(2)}) async-start(), calls=%async_computation.6 | async-start | bytes 2088960 | tf_op jit(solution)/shard_map/all_gather | solution.py:133
  234.0 137.2 %all-gather.12.cloned.1.call-start = ((), (), s32[]{:S(2)}) async-start(), calls=%async_computation.5 | async-start | bytes 2088960 | tf_op jit(solution)/shard_map/all_gather | solution.py:132
  234.6 194.3 %reduce-scatter.2.cloned.1.call-start = ((), (), s32[]{:S(2)}) async-start(), calls=%async_computation.7 | async-start | bytes 7077888 | tf_op jit(solution)/shard_map/reduce_scatter | solution.py:138
  386.8 44.3 %copy-start.1 = (bf16[1536,256]{1,0:T(8,128)(2,1)S(1)}, bf16[1536,256]{1,0:T(8,128)(2,1)}, u32[]{:S(2)}) copy-start(bf16[1536,256]{1,0:T(8,128)(2,1)} %param.17) | copy-start | bytes 2359300
Sparse Core Ops, SparseCore 0:
  20.7 26.9 all-gather.5
  50.7 139.0 all-gather.9
  233.6 45.8 all-gather.7
  281.5 43.6 all-gather.13
  327.2 43.9 all-gather.11
  387.0 41.8 reduce-scatter.1
where the time goes:
time: 444 us; the launch traced here: 438 us
  waiting for transfers between devices  269 us (61%)
  matrix products  88.4 us (20%)
  other arithmetic  35 us (8%)
  between operations  19.9 us (4%)
  local copies, waits for them, and re-layouts  16.9 us (4%)
  starting transfers between devices  9.38 us (2%)
    all_to_all x1, waiting for transfers between devices, body(): lax.all_to_all(outgoing, 'req', split_axis=0, concat_axis=0, tiled=True)  97.6 us
    all_gather x1, waiting for transfers between devices, body(): lax.all_gather(w_up, 'req', axis=0, tiled=True)  46.1 us
    all_gather x1, waiting for transfers between devices, body(): all_rows = lax.all_gather(ffn_in, 'mlp', axis=0, tiled=True)  44.8 us
    reduce_scatter x1, waiting for transfers between devices, body(): lax.psum_scatter(lax.dot_general(hidden, down_full, (((1,), (1,)), ((), (...  42 us
    all_gather x1, waiting for transfers between devices, body(): lax.all_gather(w_down, 'req', axis=0, tiled=True)  36.4 us
    reduce_sum x2, other arithmetic, attend(): return (top, jnp.sum(weights, axis=-1), mixed)  21.8 us
    dot_general x2, matrix products, attend(): jnp.einsum('thk,kd->thd', weights.astype(jnp.bfloat16), piece[:, HD:], pr...  20.5 us
    dot_general x2, matrix products, attend(): jnp.einsum('thd,kd->thk', queries, piece[:, :HD], preferred_element_type=...  19.9 us
  transfers between devices with their start and end apart: 7, of which 5 were waited for; matrix products, arithmetic and copies ran while one was open for 26% of the time, Pallas kernels for 0%

commit v1 on v0

--- a/solution.py
+++ b/solution.py
@@ -7,6 +7,28 @@
 HD = 128
 WINDOW = 1024
 EPS = 1e-06
+
+
+def joined_along(parts, dim):
+    lengths = list(parts.shape[1:])
+    lengths[dim] *= parts.shape[0]
+    return jnp.moveaxis(parts, 0, dim).reshape(lengths)
+
+
+def ring_gather(x, axis, dim):
+    peers = lax.axis_size(axis)
+    pairs = [(i, (i + 1) % peers) for i in range(peers)]
+    back = [(b, a) for a, b in pairs]
+    lower, upper = ([], [])
+    for hop in range(peers - 1):
+        if hop % 2 == 0:
+            lower.append(lax.ppermute(lower[-1] if lower else x, axis, pairs))
+        else:
+            upper.append(lax.ppermute(upper[-1] if upper else x, axis, back))
+    tiles = jnp.stack([*lower[::-1], x, *upper])
+    shift = lax.axis_index(axis) - len(lower)
+    tiles = tiles[(jnp.arange(peers) - shift) % peers]
+    return joined_along(tiles, dim)
 
 
 def rms_scale(values, gain):
@@ -130,7 +152,7 @@
     gate_full, up_full, down_full = (
         lax.all_gather(w_gate, "req", axis=0, tiled=True),
         lax.all_gather(w_up, "req", axis=0, tiled=True),
-        lax.all_gather(w_down, "req", axis=0, tiled=True),
+        ring_gather(w_down, "req", 0),
     )
     gate = jnp.dot(all_rows, gate_full, preferred_element_type=jnp.float32)
     upward = jnp.dot(all_rows, up_full, preferred_element_type=jnp.float32)

time: 444 us -> 397 us (0.89)
  waiting for transfers between devices: 269 us -> 174 us
  starting transfers between devices: 9.38 us -> 43.9 us
  local copies, waits for them, and re-layouts: 16.9 us -> 31.1 us
    all_gather x1, waiting for transfers between devices: 44.8 us -> 0.01 us  [body(): all_rows = lax.all_gather(ffn_in, 'mlp', axis=0, tiled=True)]
    all_gather x1, waiting for transfers between devices: 46.1 us -> 9.49 us  [body(): lax.all_gather(w_up, 'req', axis=0, tiled=True)]
    all_gather x1 -> x0, waiting for transfers between devices: 36.4 us -> none  [body(): lax.all_gather(w_down, 'req', axis=0, tiled=True)]
    ppermute x0 -> x15, starting transfers between devices: none -> 34.6 us  [the longest x7 34.5 us: ring_gather(): upper.append(lax.ppermute(upper[-1] if upper else x, axis, back))]
    ppermute x0 -> x15, waiting for transfers between devices: none -> 23.4 us  [the longest x8 23.4 us: ring_gather(): lower.append(lax.ppermute(lower[-1] if lower else x, axis, pairs))]
    unnamed x26 -> x45, local copies, waits for them, and re-layouts: 2.16 us -> 12.9 us
  transfers between devices with their start and end apart: 7 -> 21, of which waited for: 5 -> 11; matrix products, arithmetic and copies ran while one was open for 26% -> 33% of each run, Pallas kernels for 0% -> 0%
where the time goes in v1:
time: 397 us; the launch traced here: 391 us
  waiting for transfers between devices  174 us (44%)
  matrix products  88.2 us (22%)
  starting transfers between devices  43.9 us (11%)
  other arithmetic  34.4 us (9%)
  local copies, waits for them, and re-layouts  31.1 us (8%)
  between operations  19.7 us (5%)
    all_to_all x1, waiting for transfers between devices, body(): lax.all_to_all(outgoing, 'req', split_axis=0, concat_axis=0, tiled=True)  98.3 us
    reduce_scatter x1, waiting for transfers between devices, body(): lax.psum_scatter(lax.dot_general(hidden, down_full, (((1,), (1,)), ((), (...  42 us
    ppermute x7, starting transfers between devices, ring_gather(): upper.append(lax.ppermute(upper[-1] if upper else x, axis, back))  34.5 us
    ppermute x8, waiting for transfers between devices, ring_gather(): lower.append(lax.ppermute(lower[-1] if lower else x, axis, pairs))  23.4 us
    reduce_sum x2, other arithmetic, attend(): return (top, jnp.sum(weights, axis=-1), mixed)  21.8 us
    dot_general x2, matrix products, attend(): jnp.einsum('thk,kd->thd', weights.astype(jnp.bfloat16), piece[:, HD:], pr...  20.5 us
    dot_general x2, matrix products, attend(): jnp.einsum('thd,kd->thk', queries, piece[:, :HD], preferred_element_type=...  19.9 us
    dot_general x1, matrix products, body(): lax.dot_general(hidden, down_full, (((1,), (1,)), ((), ())), preferred_el...  15.4 us
  transfers between devices with their start and end apart: 21, of which 11 were waited for; matrix products, arithmetic and copies ran while one was open for 33% of the time, Pallas kernels for 0%

profile of v1, /device:TPU:1, one launch (start us, length us, event | category | flops | bytes accessed | tf_op | source)
XLA Modules:
  0.0 391.5 jit_solution(16163174754400368248)
XLA Ops:
  20.5 7.2 %convert_bitcast_fusion = bf16[16,2,512,256]{3,0,2,1:T(8,128)(2,1)} fusion(bf16[2,8,512,256]{3,2,1,0:T(8,128)(2,1)} %param.23, s32[16,2]{0,1:T(2,128)S(1)} %get-tuple-element.24, pred[16,2]{0,1:T(4,128)(4,1)S(1)} %fusion.54), kind=kOutput, calls=%fused_computation.16 | convolution fusion | flops 71303680 | bytes 12583072 | tf_op jit(solution)/shard_map/rln,lnsc->rlsc/dot_general | solution.py:135
  27.8 9.6 %copy.33 = bf16[16,2,512,256]{3,2,1,0:T(8,128)(2,1)} copy(bf16[16,2,512,256]{3,0,2,1:T(8,128)(2,1)} %convert_bitcast_fusion) | data formatting | bytes 16777216 | tf_op jit(solution)/shard_map/convert_element_type | solution.py:137
  37.4 8.9 %all-to-all-start = ((bf16[16,2,512,256]{3,2,1,0:T(8,128)(2,1)}), bf16[16,2,512,256]{3,2,1,0:T(8,128)(2,1)}, u32[]{:S(2)}, u32[]{:S(2)}) async-start(bf16[16,2,512,256]{3,2,1,0:T(8,128)(2,1)} %copy.33), calls=%async_computation | async-start | bytes 16777216 | tf_op jit(solution)/shard_map/all_to_all | solution.py:138
  47.4 4.3 %fusion.37 = f32[256,1536]{0,1:T(8,128)S(1)} fusion(bf16[1536,1536]{1,0:T(8,128)(2,1)} %param.16, bf16[256,1536]{1,0:T(8,128)(2,1)S(1)} %copy-done.3, f32[1536]{0:T(1024)S(1)} %copy-done.11, f32[256]{0:T(256)S(1)} %add_rsqrt_fusion.1), kind=kOutput, calls=%fused_computation.63 | convolution fusion | flops 1209532416 | bytes 7085056 | tf_op jit(solution)/shard_map/dot_general | solution.py:106
  61.0 11.8 %select_reduce_fusion = (f32[256,12]{0,1:T(8,128)S(1)}, f32[256,12,2048]{2,0,1:T(8,128)}) fusion(pred[256,2048]{1,0:T(8,128)(4,1)S(1)} %fusion.24, bf16[256,12,128]{2,0,1:T(8,128)(2,1)S(1)} %fusion.28, bf16[2048,256]{0,1:T(8,128)(2,1)} %all-gather.5.cloned.1.call-done), kind=kOutput, calls=%fused_computation.3 | convolution fusion | flops 1623192576 | bytes 27013120 | tf_op jit(solution)/shard_map/thd,kd->thk/dot_general | solution.py:51
  72.9 11.3 %fusion = f32[256,12]{0,1:T(8,128)S(1)} fusion(f32[256,12,2048]{2,0,1:T(8,128)} %get-tuple-element.27, f32[256,12]{0,1:T(8,128)S(1)} %get-tuple-element.18, pred[256,2048]{1,0:T(8,128)(4,1)S(1)} %fusion.24), kind=kLoop, calls=%fused_computation.4 | loop fusion | flops 18871296 | bytes 25714688 | tf_op jit(solution)/shard_map/reduce_sum | solution.py:63
  84.2 11.8 %fusion.4 = f32[256,12,128]{0,2,1:T(8,128)} fusion(f32[256,12,2048]{2,0,1:T(8,128)} %get-tuple-element.27, f32[256,12]{0,1:T(8,128)S(1)} %get-tuple-element.18, pred[256,2048]{1,0:T(8,128)(4,1)S(1)} %fusion.24, bf16[2048,256]{0,1:T(8,128)(2,1)S(1)} %copy-done.5), kind=kOutput, calls=%fused_computation.10 | convolution fusion | flops 1629487104 | bytes 27803648 | tf_op jit(solution)/shard_map/thk,kd->thd/dot_general | solution.py:57
  96.0 98.3 %all-to-all-done = bf16[16,2,512,256]{3,2,1,0:T(8,128)(2,1)} async-done(((bf16[16,2,512,256]{3,2,1,0:T(8,128)(2,1)}), bf16[16,2,512,256]{3,2,1,0:T(8,128)(2,1)}, u32[]{:S(2)}, u32[]{:S(2)}) %all-to-all-start) | async-done | bytes 8388640 | tf_op jit(solution)/shard_map/all_to_all | solution.py:138
  194.3 8.3 %fusion.10 = bf16[2,1,512,256]{3,1,2,0:T(2,128)(2,1)S(1)} fusion(pred[16,2,1,1]{0,2,3,1:T(4,128)(4,1)S(1)} %copy.38, bf16[16,2,512,256]{3,2,1,0:T(8,128)(2,1)} %all-to-all-done), kind=kOutput, calls=%fused_computation.14 | convolution fusion | flops 8388608 | bytes 8912928 | tf_op jit(solution)/shard_map/rl,rlsc->lsc/dot_general | solution.py:139
  203.6 8.1 %select_reduce_fusion.1 = (f32[256,12]{0,1:T(8,128)S(1)}, f32[256,12,1536]{2,0,1:T(8,128)}) fusion(pred[256,1536]{1,0:T(8,128)(4,1)S(1)} %fusion.30, bf16[256,12,128]{2,0,1:T(8,128)(2,1)S(1)} %fusion.28, bf16[1536,256]{1,0:T(8,128)(2,1)S(1)} %pad_maximum_fusion), kind=kOutput, calls=%fused_computation.7 | convolution fusion | flops 1217393664 | bytes 20459520 | tf_op jit(solution)/shard_map/thd,kd->thk/dot_general | solution.py:51
  211.7 10.5 %fusion.2 = f32[256,12]{0,1:T(8,128)S(1)} fusion(f32[256,12,1536]{2,0,1:T(8,128)} %get-tuple-element.29, f32[256,12]{0,1:T(8,128)S(1)} %is-finite_select_fusion, pred[256,1536]{1,0:T(8,128)(4,1)S(1)} %fusion.30), kind=kLoop, calls=%fused_computation.8 | loop fusion | flops 14152704 | bytes 19292160 | tf_op jit(solution)/shard_map/reduce_sum | solution.py:63
  222.3 8.7 %divide_convert_fusion = bf16[256,12,128]{0,2,1:T(8,128)(2,1)S(1)} fusion(f32[256,12,128]{0,2,1:T(8,128)} %fusion.4, f32[256,12,1536]{2,0,1:T(8,128)} %get-tuple-element.29, f32[256,12]{0,1:T(8,128)S(1)} %is-finite_select_fusion, pred[256,1536]{1,0:T(8,128)(4,1)S(1)} %fusion.30, f32[256,12]{0,1:T(8,128)S(1)} %get-tuple-element.5, ...), kind=kOutput, calls=%fused_computation.47 | convolution fusion | flops 1224867840 | bytes 22118400 | tf_op jit(solution)/shard_map/thk,kd->thd/dot_general | solution.py:57
  233.9 7.0 %collective-permute-done = bf16[96,576]{1,0:T(8,128)(2,1)S(1)} collective-permute-done((bf16[96,576]{1,0:T(8,128)(2,1)S(1)}, bf16[96,576]{1,0:T(8,128)(2,1)S(1)}, u32[]{:S(2)}, u32[]{:S(2)}) %collective-permute-start) | collective-permute-done | bytes 110624 | tf_op jit(solution)/shard_map/ppermute | solution.py:25
  240.9 4.8 %collective-permute-start.8 = (bf16[96,576]{1,0:T(8,128)(2,1)S(1)}, bf16[96,576]{1,0:T(8,128)(2,1)S(1)}, u32[]{:S(2)}, u32[]{:S(2)}) collective-permute-start(bf16[96,576]{1,0:T(8,128)(2,1)S(1)} %copy-done.7), channel_id=1, source_target_pairs={{8,0},{16,8},{24,16},{32,24},{40,32},{48,40},{56,48},{64,56},{72,6... | collective-permute-start | bytes 331784 | tf_op jit(solution)/shard_map/ppermute | solution.py:27
  245.7 2.3 collective-permute-done.1
  248.0 4.8 %collective-permute-start.9 = (bf16[96,576]{1,0:T(8,128)(2,1)S(1)}, bf16[96,576]{1,0:T(8,128)(2,1)S(1)}, u32[]{:S(2)}, u32[]{:S(2)}) collective-permute-start(bf16[96,576]{1,0:T(8,128)(2,1)S(1)} %collective-permute-done.8), channel_id=1, source_target_pairs={{8,0},{16,8},{24,16},{32,24},{40,32},{48,40},{56,48},{64,56},{72,6... | collective-permute-start | bytes 331784 | tf_op jit(solution)/shard_map/ppermute | solution.py:27
  252.7 2.3 collective-permute-done.2
  255.0 4.8 %collective-permute-start.10 = (bf16[96,576]{1,0:T(8,128)(2,1)S(1)}, bf16[96,576]{1,0:T(8,128)(2,1)S(1)}, u32[]{:S(2)}, u32[]{:S(2)}) collective-permute-start(bf16[96,576]{1,0:T(8,128)(2,1)S(1)} %collective-permute-done.9), channel_id=1, source_target_pairs={{8,0},{16,8},{24,16},{32,24},{40,32},{48,40},{56,48},{64,56},{72,6... | collective-permute-start | bytes 331784 | tf_op jit(solution)/shard_map/ppermute | solution.py:27
  259.8 2.3 collective-permute-done.3
  262.1 4.8 %collective-permute-start.11 = (bf16[96,576]{1,0:T(8,128)(2,1)S(1)}, bf16[96,576]{1,0:T(8,128)(2,1)S(1)}, u32[]{:S(2)}, u32[]{:S(2)}) collective-permute-start(bf16[96,576]{1,0:T(8,128)(2,1)S(1)} %collective-permute-done.10), channel_id=1, source_target_pairs={{8,0},{16,8},{24,16},{32,24},{40,32},{48,40},{56,48},{64,56},{72,6... | collective-permute-start | bytes 331784 | tf_op jit(solution)/shard_map/ppermute | solution.py:27
  266.9 2.3 collective-permute-done.4
  269.2 4.9 %collective-permute-start.12 = (bf16[96,576]{1,0:T(8,128)(2,1)S(1)}, bf16[96,576]{1,0:T(8,128)(2,1)S(1)}, u32[]{:S(2)}, u32[]{:S(2)}) collective-permute-start(bf16[96,576]{1,0:T(8,128)(2,1)S(1)} %collective-permute-done.11), channel_id=1, source_target_pairs={{8,0},{16,8},{24,16},{32,24},{40,32},{48,40},{56,48},{64,56},{72,6... | collective-permute-start | bytes 331784 | tf_op jit(solution)/shard_map/ppermute | solution.py:27
  274.1 3.0 collective-permute-done.5
  277.1 5.2 %collective-permute-start.13 = (bf16[96,576]{1,0:T(8,128)(2,1)S(1)}, bf16[96,576]{1,0:T(8,128)(2,1)S(1)}, u32[]{:S(2)}, u32[]{:S(2)}) collective-permute-start(bf16[96,576]{1,0:T(8,128)(2,1)S(1)} %collective-permute-done.12), channel_id=1, source_target_pairs={{8,0},{16,8},{24,16},{32,24},{40,32},{48,40},{56,48},{64,56},{72,6... | collective-permute-start | bytes 331784 | tf_op jit(solution)/shard_map/ppermute | solution.py:27
  282.3 2.6 collective-permute-done.6
  285.0 5.3 %collective-permute-start.14 = (bf16[96,576]{1,0:T(8,128)(2,1)S(1)}, bf16[96,576]{1,0:T(8,128)(2,1)S(1)}, u32[]{:S(2)}, u32[]{:S(2)}) collective-permute-start(bf16[96,576]{1,0:T(8,128)(2,1)S(1)} %collective-permute-done.13), channel_id=1, source_target_pairs={{8,0},{16,8},{24,16},{32,24},{40,32},{48,40},{56,48},{64,56},{72,6... | collective-permute-start | bytes 331784 | tf_op jit(solution)/shard_map/ppermute | solution.py:27
  302.5 3.6 gather_fusion.1
  306.2 9.3 %fusion.65 = f32[2048,576]{0,1:T(8,128)} fusion(bf16[2048,1536]{1,0:T(8,128)(2,1)} %all-gather.7.cloned.1.call-done, bf16[1536,576]{1,0:T(8,128)(2,1)} %all-gather.9.cloned.1.call-done), kind=kOutput, calls=%fused_computation.157 | convolution fusion | flops 3623878656 | bytes 12779520 | tf_op jit(solution)/shard_map/dot_general | solution.py:157
  315.5 9.5 %all-gather.11.cloned.1.call-done = bf16[1536,576]{1,0:T(8,128)(2,1)} async-done(((bf16[96,576]{1,0:T(8,128)(2,1)}), bf16[1536,576]{1,0:T(8,128)(2,1)}) %all-gather.11.cloned.1.call-update) | async-done | bytes 1769488 | tf_op jit(solution)/shard_map/all_gather | solution.py:154
  325.0 15.4 %convolution_convert_fusion = bf16[2048,1536]{1,0:T(8,128)(2,1)} fusion(bf16[1536,576]{1,0:T(8,128)(2,1)} %bitcast.97, f32[2048,576]{0,1:T(8,128)} %fusion.65, bf16[2048,1536]{1,0:T(8,128)(2,1)} %all-gather.7.cloned.1.call-done, bf16[1536,576]{1,0:T(8,128)(2,1)} %all-gather.11.cloned.1.call-done), kind=kOutput, calls=%fused_computation.17 | convolution fusion | flops 7262699520 | bytes 20840448 | tf_op jit(solution)/shard_map/dot_general | solution.py:161
  340.5 42.0 %reduce-scatter.2.cloned.1.call-done = bf16[256,1536]{1,0:T(8,128)(2,1)} async-done(((bf16[2048,1536]{1,0:T(8,128)(2,1)}), bf16[256,1536]{1,0:T(8,128)(2,1)}) %reduce-scatter.2.cloned.1.call-update) | async-done | bytes 786448 | tf_op jit(solution)/shard_map/reduce_scatter | solution.py:160
  382.5 2.2 add_convert_fusion
  (122 shorter events, 34.5 us)
Async XLA Ops:
  6.5 7.2 %copy-start = (bf16[1536,256]{1,0:T(8,128)(2,1)S(1)}, bf16[1536,256]{1,0:T(8,128)(2,1)}, u32[]{:S(2)}) copy-start(bf16[1536,256]{1,0:T(8,128)(2,1)} %param.17) | copy-start | bytes 2359300
  6.5 9.6 %copy-start.10 = (s32[3,128]{1,0:T(4,128)S(1)}, s32[3,128]{1,0:T(4,128)}, u32[]{:S(2)}) copy-start(s32[3,128]{1,0:T(4,128)} %param.27) | copy-start | bytes 4612
  6.5 54.5 %all-gather.5.cloned.1.call-start = ((), (), s32[]{:S(2)}) async-start(), calls=%async_computation.2 | async-start | bytes 1179648 | tf_op jit(solution)/shard_map/all_gather | solution.py:119
  12.4 7.4 %copy-start.9 = (s32[16]{0:T(128)S(1)}, s32[16]{0:T(128)}, u32[]{:S(2)}) copy-start(s32[16]{0:T(128)} %param.25) | copy-start | bytes 196
  12.4 7.4 %copy-start.2 = (s32[128]{0:T(128)S(1)}, s32[128]{0:T(128)}, u32[]{:S(2)}) copy-start(s32[128]{0:T(128)} %param.26) | copy-start | bytes 1540
  37.4 10.0 %copy-start.3 = (bf16[256,1536]{1,0:T(8,128)(2,1)S(1)}, bf16[256,1536]{1,0:T(8,128)(2,1)}, u32[]{:S(2)}) copy-start(bf16[256,1536]{1,0:T(8,128)(2,1)} %param.14) | copy-start | bytes 2359300
  37.4 10.0 %copy-start.11 = (f32[1536]{0:T(1024)S(1)}, f32[1536]{0:T(1024)}, u32[]{:S(2)}) copy-start(f32[1536]{0:T(1024)} %param.15) | copy-start | bytes 18436
  37.4 157.0 %all-to-all-start = ((bf16[16,2,512,256]{3,2,1,0:T(8,128)(2,1)}), bf16[16,2,512,256]{3,2,1,0:T(8,128)(2,1)}, u32[]{:S(2)}, u32[]{:S(2)}) async-start(bf16[16,2,512,256]{3,2,1,0:T(8,128)(2,1)} %copy.33), calls=%async_computation | async-start | bytes 16777216 | tf_op jit(solution)/shard_map/all_to_all | solution.py:138
  46.2 259.9 %all-gather.9.cloned.1.call-start = ((), (), s32[]{:S(2)}) async-start(), calls=%async_computation.4 | async-start | bytes 2088960 | tf_op jit(solution)/shard_map/all_gather | solution.py:153
  47.0 259.2 %all-gather.7.cloned.1.call-start = ((), (), s32[]{:S(2)}) async-start(), calls=%async_computation.3 | async-start | bytes 7077888 | tf_op jit(solution)/shard_map/all_gather | solution.py:151
  72.9 11.4 %copy-start.5 = (bf16[2048,256]{0,1:T(8,128)(2,1)S(1)}, bf16[2048,256]{0,1:T(8,128)(2,1)}, u32[]{:S(2)}) copy-start(bf16[2048,256]{0,1:T(8,128)(2,1)} %all-gather.5.cloned.1.call-done) | copy-start | bytes 3145732
  211.7 19.3 %slice-start = ((s8[4718592]{0:T(1024)(128)(4,1)}), s8[524288]{0:T(1024)(128)(4,1)S(1)}, s32[]{:S(2)}) async-start(s8[4718592]{0:T(1024)(128)(4,1)} %bitcast.93), calls=%async_computation.7 | async-start | bytes 1048576
  222.3 8.8 %slice-start.1 = ((s8[4718592]{0:T(1024)(128)(4,1)}), s8[4194304]{0:T(1024)(128)(4,1)S(1)}, s32[]{:S(2)}) async-start(s8[4718592]{0:T(1024)(128)(4,1)} %bitcast.93), calls=%async_computation.8 | async-start | bytes 8388608
  222.3 8.8 %copy-start.4 = (bf16[256,1536]{1,0:T(8,128)(2,1)S(1)}, bf16[256,1536]{1,0:T(8,128)(2,1)}, u32[]{:S(2)}) copy-start(bf16[256,1536]{1,0:T(8,128)(2,1)} %param.14) | copy-start | bytes 2359300
  233.7 91.3 %all-gather.11.cloned.1.call-start = ((), (), s32[]{:S(2)}) async-start(), calls=%async_computation.5 | async-start | bytes 2088960 | tf_op jit(solution)/shard_map/all_gather | solution.py:154
  233.8 7.1 %collective-permute-start = (bf16[96,576]{1,0:T(8,128)(2,1)S(1)}, bf16[96,576]{1,0:T(8,128)(2,1)S(1)}, u32[]{:S(2)}, u32[]{:S(2)}) collective-permute-start(bf16[96,576]{1,0:T(8,128)(2,1)S(1)} %copy-done.7), channel_id=1, source_target_pairs={{0,8},{8,16},{16,24},{24,32},{32,40},{40,48},{48,56},{56,64},{64,7... | collective-permute-start | bytes 331784 | tf_op jit(solution)/shard_map/ppermute | solution.py:25
  240.9 7.1 %collective-permute-start.1 = (bf16[96,576]{1,0:T(8,128)(2,1)S(1)}, bf16[96,576]{1,0:T(8,128)(2,1)S(1)}, u32[]{:S(2)}, u32[]{:S(2)}) collective-permute-start(bf16[96,576]{1,0:T(8,128)(2,1)S(1)} %collective-permute-done), channel_id=1, source_target_pairs={{0,8},{8,16},{16,24},{24,32},{32,40},{40,48},{48,56},{56,64},{64,7... | collective-permute-start | bytes 331784 | tf_op jit(solution)/shard_map/ppermute | solution.py:25
  240.9 7.1 %collective-permute-start.8 = (bf16[96,576]{1,0:T(8,128)(2,1)S(1)}, bf16[96,576]{1,0:T(8,128)(2,1)S(1)}, u32[]{:S(2)}, u32[]{:S(2)}) collective-permute-start(bf16[96,576]{1,0:T(8,128)(2,1)S(1)} %copy-done.7), channel_id=1, source_target_pairs={{8,0},{16,8},{24,16},{32,24},{40,32},{48,40},{56,48},{64,56},{72,6... | collective-permute-start | bytes 331784 | tf_op jit(solution)/shard_map/ppermute | solution.py:27
  248.0 7.1 %collective-permute-start.2 = (bf16[96,576]{1,0:T(8,128)(2,1)S(1)}, bf16[96,576]{1,0:T(8,128)(2,1)S(1)}, u32[]{:S(2)}, u32[]{:S(2)}) collective-permute-start(bf16[96,576]{1,0:T(8,128)(2,1)S(1)} %collective-permute-done.1), channel_id=1, source_target_pairs={{0,8},{8,16},{16,24},{24,32},{32,40},{40,48},{48,56},{56,64},{64,7... | collective-permute-start | bytes 331784 | tf_op jit(solution)/shard_map/ppermute | solution.py:25
  248.0 7.1 %collective-permute-start.9 = (bf16[96,576]{1,0:T(8,128)(2,1)S(1)}, bf16[96,576]{1,0:T(8,128)(2,1)S(1)}, u32[]{:S(2)}, u32[]{:S(2)}) collective-permute-start(bf16[96,576]{1,0:T(8,128)(2,1)S(1)} %collective-permute-done.8), channel_id=1, source_target_pairs={{8,0},{16,8},{24,16},{32,24},{40,32},{48,40},{56,48},{64,56},{72,6... | collective-permute-start | bytes 331784 | tf_op jit(solution)/shard_map/ppermute | solution.py:27
  255.0 7.1 %collective-permute-start.3 = (bf16[96,576]{1,0:T(8,128)(2,1)S(1)}, bf16[96,576]{1,0:T(8,128)(2,1)S(1)}, u32[]{:S(2)}, u32[]{:S(2)}) collective-permute-start(bf16[96,576]{1,0:T(8,128)(2,1)S(1)} %collective-permute-done.2), channel_id=1, source_target_pairs={{0,8},{8,16},{16,24},{24,32},{32,40},{40,48},{48,56},{56,64},{64,7... | collective-permute-start | bytes 331784 | tf_op jit(solution)/shard_map/ppermute | solution.py:25
  255.0 7.1 %collective-permute-start.10 = (bf16[96,576]{1,0:T(8,128)(2,1)S(1)}, bf16[96,576]{1,0:T(8,128)(2,1)S(1)}, u32[]{:S(2)}, u32[]{:S(2)}) collective-permute-start(bf16[96,576]{1,0:T(8,128)(2,1)S(1)} %collective-permute-done.9), channel_id=1, source_target_pairs={{8,0},{16,8},{24,16},{32,24},{40,32},{48,40},{56,48},{64,56},{72,6... | collective-permute-start | bytes 331784 | tf_op jit(solution)/shard_map/ppermute | solution.py:27
  262.1 7.1 %collective-permute-start.4 = (bf16[96,576]{1,0:T(8,128)(2,1)S(1)}, bf16[96,576]{1,0:T(8,128)(2,1)S(1)}, u32[]{:S(2)}, u32[]{:S(2)}) collective-permute-start(bf16[96,576]{1,0:T(8,128)(2,1)S(1)} %collective-permute-done.3), channel_id=1, source_target_pairs={{0,8},{8,16},{16,24},{24,32},{32,40},{40,48},{48,56},{56,64},{64,7... | collective-permute-start | bytes 331784 | tf_op jit(solution)/shard_map/ppermute | solution.py:25
  262.1 7.1 %collective-permute-start.11 = (bf16[96,576]{1,0:T(8,128)(2,1)S(1)}, bf16[96,576]{1,0:T(8,128)(2,1)S(1)}, u32[]{:S(2)}, u32[]{:S(2)}) collective-permute-start(bf16[96,576]{1,0:T(8,128)(2,1)S(1)} %collective-permute-done.10), channel_id=1, source_target_pairs={{8,0},{16,8},{24,16},{32,24},{40,32},{48,40},{56,48},{64,56},{72,6... | collective-permute-start | bytes 331784 | tf_op jit(solution)/shard_map/ppermute | solution.py:27
  269.1 8.0 %collective-permute-start.5 = (bf16[96,576]{1,0:T(8,128)(2,1)S(1)}, bf16[96,576]{1,0:T(8,128)(2,1)S(1)}, u32[]{:S(2)}, u32[]{:S(2)}) collective-permute-start(bf16[96,576]{1,0:T(8,128)(2,1)S(1)} %collective-permute-done.4), channel_id=1, source_target_pairs={{0,8},{8,16},{16,24},{24,32},{32,40},{40,48},{48,56},{56,64},{64,7... | collective-permute-start | bytes 331784 | tf_op jit(solution)/shard_map/ppermute | solution.py:25
  269.1 113.4 %reduce-scatter.2.cloned.1.call-start = ((), (), s32[]{:S(2)}) async-start(), calls=%async_computation.6 | async-start | bytes 7077888 | tf_op jit(solution)/shard_map/reduce_scatter | solution.py:160
  269.2 7.9 %collective-permute-start.12 = (bf16[96,576]{1,0:T(8,128)(2,1)S(1)}, bf16[96,576]{1,0:T(8,128)(2,1)S(1)}, u32[]{:S(2)}, u32[]{:S(2)}) collective-permute-start(bf16[96,576]{1,0:T(8,128)(2,1)S(1)} %collective-permute-done.11), channel_id=1, source_target_pairs={{8,0},{16,8},{24,16},{32,24},{40,32},{48,40},{56,48},{64,56},{72,6... | collective-permute-start | bytes 331784 | tf_op jit(solution)/shard_map/ppermute | solution.py:27
  277.1 7.9 %collective-permute-start.6 = (bf16[96,576]{1,0:T(8,128)(2,1)S(1)}, bf16[96,576]{1,0:T(8,128)(2,1)S(1)}, u32[]{:S(2)}, u32[]{:S(2)}) collective-permute-start(bf16[96,576]{1,0:T(8,128)(2,1)S(1)} %collective-permute-done.5), channel_id=1, source_target_pairs={{0,8},{8,16},{16,24},{24,32},{32,40},{40,48},{48,56},{56,64},{64,7... | collective-permute-start | bytes 331784 | tf_op jit(solution)/shard_map/ppermute | solution.py:25
  277.1 7.9 %collective-permute-start.13 = (bf16[96,576]{1,0:T(8,128)(2,1)S(1)}, bf16[96,576]{1,0:T(8,128)(2,1)S(1)}, u32[]{:S(2)}, u32[]{:S(2)}) collective-permute-start(bf16[96,576]{1,0:T(8,128)(2,1)S(1)} %collective-permute-done.12), channel_id=1, source_target_pairs={{8,0},{16,8},{24,16},{32,24},{40,32},{48,40},{56,48},{64,56},{72,6... | collective-permute-start | bytes 331784 | tf_op jit(solution)/shard_map/ppermute | solution.py:27
  284.9 7.1 %collective-permute-start.7 = (bf16[96,576]{1,0:T(8,128)(2,1)S(1)}, bf16[96,576]{1,0:T(8,128)(2,1)S(1)}, u32[]{:S(2)}, u32[]{:S(2)}) collective-permute-start(bf16[96,576]{1,0:T(8,128)(2,1)S(1)} %collective-permute-done.6), channel_id=1, source_target_pairs={{0,8},{8,16},{16,24},{24,32},{32,40},{40,48},{48,56},{56,64},{64,7... | collective-permute-start | bytes 331784 | tf_op jit(solution)/shard_map/ppermute | solution.py:25
  285.0 16.9 %collective-permute-start.14 = (bf16[96,576]{1,0:T(8,128)(2,1)S(1)}, bf16[96,576]{1,0:T(8,128)(2,1)S(1)}, u32[]{:S(2)}, u32[]{:S(2)}) collective-permute-start(bf16[96,576]{1,0:T(8,128)(2,1)S(1)} %collective-permute-done.13), channel_id=1, source_target_pairs={{8,0},{16,8},{24,16},{32,24},{40,32},{48,40},{56,48},{64,56},{72,6... | collective-permute-start | bytes 331784 | tf_op jit(solution)/shard_map/ppermute | solution.py:27
  340.5 44.2 %copy-start.1 = (bf16[1536,256]{1,0:T(8,128)(2,1)S(1)}, bf16[1536,256]{1,0:T(8,128)(2,1)}, u32[]{:S(2)}) copy-start(bf16[1536,256]{1,0:T(8,128)(2,1)} %param.17) | copy-start | bytes 2359300
  (3 other events, 3.7 us)
Sparse Core Ops, SparseCore 0:
  19.9 26.9 all-gather.4
  49.3 139.3 all-gather.8
  233.8 45.4 all-gather.6
  281.3 43.6 all-gather.10
  340.6 41.8 reduce-scatter.1
